TPU v7x, 32 devices: a whole 2x2x4 slice. The times are simulated.
32 devices in a mesh: section: 2 (over x), seq: 8 (over z, y), head: 2 (over core).
Axes of the slice: x: 2, y: 2, z: 4, core: 2. Of those that a mesh axis runs over, the one named last changes fastest.
Arguments:
- bwd_input: bfloat16 [2, 1024, 3584], P('section', 'seq', 'head'), may hold values from -6 to 6
- bwd_docs: int32 [2, 1024], P('section', 'seq'), may hold values from 0 to 3, as said below
- bwd_grad: bfloat16 [2, 1024, 3584], P('section', 'seq', 'head'), may hold values from -6 to 6
- proj_weight: bfloat16 [2, 256, 3584], P('section', 'seq', 'head'), may hold values from -0.09375 to 0.09375
- step_weight: float32 [2, 3584], P('section', 'head'), may hold values from -0.75 to 0.75
- step_bias: float32 [2, 56], P('section', 'head'), may hold values from -5 to -2
- rate_log: float32 [2, 56], P('section', 'head'), may hold values from -4 to 0.5
- skip_gain: float32 [2, 56], P('section', 'head'), may hold values from 0.5 to 1.5
Outputs:
- prev_grad: bfloat16 [2, 1024, 3584], P('section', 'seq', 'head')
- grad_proj: float32 [2, 256, 3584], P('section', 'seq', 'head')
- grad_step_weight: float32 [2, 3584], P('section', 'head')
- grad_step_bias: float32 [2, 56], P('section', 'head')
- grad_rate_log: float32 [2, 56], P('section', 'head')
- grad_skip: float32 [2, 56], P('section', 'head')
Inputs may be any that keep to these rules, and one draw needn't show every extreme that they name: `bwd_docs`: document ids of each row never fall, start at 0, every id occurs, and one document of each row holds 512 tokens.
All inputs are finite; a program needn't handle non-finite values.
Results may differ from a plain program's by a relative error of at most 0.023.
Values may be sent and summed in bfloat16 or wider, within the bound.
No kernel may reach another device: no remote copies, remote signals or barrier semaphores. Data moves between devices by JAX's collectives and lax.ppermute only.
A program may use at most 64 MiB of HBM per device.

v0:
```python
import jax
import jax.numpy as jnp
from jax import lax
from jax.sharding import PartitionSpec as P

EXACT = lax.Precision.HIGHEST


def shifted(block, axis, distance):
    devices = range(lax.axis_size(axis))
    route = [(i - distance, i) for i in devices if i - distance in devices]
    return lax.ppermute(block, axis, route)


def entering(value, axis, combine, identity):
    size, mine = (lax.axis_size(axis), lax.axis_index(axis))
    everything = jax.tree.map(
        lambda part, kind: lax.all_gather(part.astype(kind), axis),
        value,
        (jnp.bfloat16, jnp.bfloat16),
    )
    start = jax.tree.map(
        lambda part, zero: jnp.broadcast_to(jnp.asarray(zero, part.dtype), part.shape),
        value,
        identity,
    )

    def lap(k, before):
        reached = k < mine
        new = combine(
            before, jax.tree.map(lambda part, own: part[k].astype(own.dtype), everything, value)
        )
        return jax.tree.map(lambda a, b: jnp.where(reached, a, b), new, before)

    return lax.fori_loop(0, size, lap, start)


def entering_2(value, axis, combine, identity):
    size, mine = (lax.axis_size(axis), lax.axis_index(axis))
    everything = jax.tree.map(
        lambda part, kind: lax.all_gather(part.astype(kind), axis),
        value,
        jax.tree.map(lambda a: jnp.bfloat16 if a.dtype == jnp.float32 else a.dtype, value),
    )
    start = jax.tree.map(
        lambda part, zero: jnp.broadcast_to(jnp.asarray(zero, part.dtype), part.shape),
        value,
        identity,
    )

    def lap(k, before):
        at = size - 1 - k
        reached = at > mine
        new = combine(
            before, jax.tree.map(lambda part, own: part[at].astype(own.dtype), everything, value)
        )
        return jax.tree.map(lambda a, b: jnp.where(reached, a, b), new, before)

    return lax.fori_loop(0, size, lap, start)


def contract(spec, left, right):
    return jnp.einsum(spec, left, right, preferred_element_type=jnp.float32)


def local_setup(values, step_weight, step_bias, rate_log):
    tokens = values.shape[0]
    raw_step = (
        jnp.einsum("thp,hp->th", values.astype(jnp.float32), step_weight, precision=EXACT)
        + step_bias[None, :]
    )
    step_size = jax.nn.softplus(raw_step)
    decay_log = -jnp.exp(rate_log)[None, :] * step_size
    row_ids = lax.broadcasted_iota(jnp.int32, (tokens, tokens), 0)
    col_ids = lax.broadcasted_iota(jnp.int32, (tokens, tokens), 1)
    triangle = (row_ids >= col_ids).astype(jnp.float32)
    cumulative = jnp.dot(triangle, decay_log, precision=EXACT)
    return (step_size, cumulative, row_ids, col_ids)


def span_summary(values, mixer, step_weight, step_bias, rate_log, docs, doc_before):
    step_size, cumulative, row_ids, col_ids = local_setup(values, step_weight, step_bias, rate_log)
    final_log = cumulative[-1]
    tail_mask = (docs == docs[-1]).astype(jnp.float32)[:, None]
    tail_weight = (
        jnp.exp(jnp.where(tail_mask > 0, final_log[None, :] - cumulative, 0.0))
        * tail_mask
        * step_size
    )
    unbroken = (docs[-1] == doc_before).astype(jnp.float32)
    carry_decay = jnp.exp(final_log) * unbroken
    half_width = mixer.shape[1] // 2
    writers = mixer[:, :half_width]
    weighted = (tail_weight[:, :, None] * writers.astype(jnp.float32)[:, None, :]).astype(
        jnp.bfloat16
    )
    span_state = contract("thn,thp->hnp", weighted, values)
    return (carry_decay, span_state)


def span_output(
    values, mixer, step_weight, step_bias, rate_log, skip_gain, docs, doc_before, incoming
):
    step_size, cumulative, row_ids, col_ids = local_setup(values, step_weight, step_bias, rate_log)
    half_width = mixer.shape[1] // 2
    writers = mixer[:, :half_width]
    readers = mixer[:, half_width:]
    affinity = jnp.dot(readers, writers.T, preferred_element_type=jnp.float32)
    same_doc = ((docs[:, None] == docs[None, :]) & (row_ids >= col_ids)).astype(jnp.float32)
    heads_first = cumulative.T
    log_gap = heads_first[:, :, None] - heads_first[:, None, :]
    mixing = (
        jnp.exp(jnp.where(same_doc[None] > 0, log_gap, 0.0))
        * same_doc[None]
        * affinity[None]
        * step_size.T[:, None, :]
    )
    mixing = mixing.astype(jnp.bfloat16)
    local_part = contract("hts,shp->thp", mixing, values)
    unbroken = (docs == doc_before).astype(jnp.float32)
    carry_scale = jnp.exp(cumulative) * unbroken[:, None]
    carried = jnp.einsum("tn,hnp->thp", readers.astype(jnp.float32), incoming, precision=EXACT)
    combined = (
        values.astype(jnp.float32) * (1.0 + skip_gain)[None, :, None]
        + local_part
        + carry_scale[:, :, None] * carried
    )
    return combined.astype(jnp.bfloat16)


def carry_join(earlier, later):
    return (earlier[0] * later[0], later[0][:, None] * earlier[1] + later[1])


def back_join(earlier, later):
    return (earlier[0] * later[0], later[1] + later[0][:, None] * earlier[1])


def shards(bwd_input, bwd_docs, bwd_grad, proj_weight, step_weight, step_bias, rate_log, skip_gain):
    tokens = bwd_input.shape[1]
    channels_here = bwd_input.shape[2]
    heads_here = step_bias.shape[1]
    head_width = channels_here // heads_here
    bwd_flat = bwd_input[0]
    bwd_values = bwd_flat.reshape(tokens, heads_here, head_width)
    weight_heads = step_weight[0].reshape(heads_here, head_width)
    bias_heads = step_bias[0]
    rate_heads = rate_log[0]
    skip_heads = skip_gain[0]
    docs_bwd = bwd_docs[0]
    doc_before = shifted(docs_bwd[-1:], "seq", 1)[0]
    full_weight = lax.all_gather(proj_weight[0], "seq", axis=0, tiled=True)
    partial_value = jnp.dot(bwd_flat, full_weight.T, preferred_element_type=jnp.float32)
    mixer_bwd = lax.psum_scatter(
        partial_value.astype(jnp.bfloat16), "head", scatter_dimension=1, tiled=True
    )

    def summary_bwd(values_in, mixer_in, weight_in, bias_in, rate_in):
        return span_summary(values_in, mixer_in, weight_in, bias_in, rate_in, docs_bwd, doc_before)

    summary_out, summary_pull = jax.vjp(
        summary_bwd, bwd_values, mixer_bwd, weight_heads, bias_heads, rate_heads
    )
    decay_bwd, state_bwd = summary_out
    state_shape = state_bwd.shape
    state_flat = state_bwd.reshape(heads_here, -1)
    seeds = (jnp.ones_like(decay_bwd), jnp.zeros_like(state_flat))
    incoming_flat = entering((decay_bwd, state_flat), "seq", carry_join, seeds)[1]
    incoming_bwd = incoming_flat.reshape(state_shape)

    def output_bwd(values_in, mixer_in, weight_in, bias_in, rate_in, skip_in, state_in):
        return span_output(
            values_in,
            mixer_in,
            weight_in,
            bias_in,
            rate_in,
            skip_in,
            docs_bwd,
            doc_before,
            state_in,
        )

    unused, output_pull = jax.vjp(
        output_bwd,
        bwd_values,
        mixer_bwd,
        weight_heads,
        bias_heads,
        rate_heads,
        skip_heads,
        incoming_bwd,
    )
    cotangent = bwd_grad[0].reshape(tokens, heads_here, head_width)
    out_grads = output_pull(cotangent)
    state_grad = out_grads[6].reshape(heads_here, -1)
    back_seeds = (jnp.ones_like(decay_bwd), jnp.zeros_like(state_grad))
    adjoint_flat = entering_2((decay_bwd, state_grad), "seq", back_join, back_seeds)[1]
    decay_grad = jnp.sum(adjoint_flat * incoming_flat, axis=1)
    sum_grads = summary_pull((decay_grad, adjoint_flat.reshape(state_shape)))
    mixer_grad = (out_grads[1].astype(jnp.float32) + sum_grads[1].astype(jnp.float32)).astype(
        jnp.bfloat16
    )
    mixer_full = lax.all_gather(mixer_grad, "head", axis=1, tiled=True)
    back_proj = jnp.dot(mixer_full, full_weight, preferred_element_type=jnp.float32)
    value_grad = (out_grads[0].astype(jnp.float32) + sum_grads[0].astype(jnp.float32)).reshape(
        tokens, channels_here
    ) + back_proj
    value_grad = value_grad.astype(jnp.bfloat16)
    prev_part = shifted(value_grad.reshape(1, tokens, channels_here), "section", -1)
    grad_rows = lax.psum_scatter(
        lax.dot_general(
            mixer_full, bwd_flat, (((0,), (0,)), ((), ())), preferred_element_type=jnp.float32
        ).astype(jnp.bfloat16),
        "seq",
        scatter_dimension=0,
        tiled=True,
    ).astype(jnp.float32)
    totals = lax.psum(
        (
            (out_grads[2] + sum_grads[2]).reshape(channels_here),
            out_grads[3] + sum_grads[3],
            out_grads[4] + sum_grads[4],
            out_grads[5],
        ),
        "seq",
    )
    return (
        prev_part,
        grad_rows[None],
        totals[0][None],
        totals[1][None],
        totals[2][None],
        totals[3][None],
    )


def solution(mesh):
    in_specs = (
        P("section", "seq", "head"),
        P("section", "seq"),
        P("section", "seq", "head"),
        P("section", "seq", "head"),
        P("section", "head"),
        P("section", "head"),
        P("section", "head"),
        P("section", "head"),
    )
    out_specs = (
        P("section", "seq", "head"),
        P("section", "seq", "head"),
        P("section", "head"),
        P("section", "head"),
        P("section", "head"),
        P("section", "head"),
    )
    return jax.shard_map(shards, mesh=mesh, in_specs=in_specs, out_specs=out_specs, check_vma=False)
```

profile of v0, /device:TPU:0, one launch (start us, length us, event | category | flops | bytes accessed | tf_op | source)
XLA Modules:
  0.0 258.4 jit_solution(6643911628214129203)
XLA Ops:
  7.2 1.3 slice.21
  8.5 5.4 %collective-permute-start = (s32[1]{0:T(128)}, s32[1]{0:T(128)}, u32[]{:S(2)}, u32[]{:S(2)}) collective-permute-start(s32[1]{0:T(128)} %bitcast.17), channel_id=1, source_target_pairs={{0,2},{2,4},{4,6},{6,8},{8,10},{10,12},{12,14},{1,3},{3,5},{5,7},{... | collective-permute-start | bytes 20 | tf_op jit(solution)/shard_map/ppermute | solution.py:12
  13.9 32.6 %all-gather = bf16[1,256,1792]{2,1,0:T(8,128)(2,1)S(1)} all-gather(bf16[1,32,1792]{2,1,0:T(8,128)(2,1)} %param.16), channel_id=2, replica_groups=mesh['section'=2,'seq'=8,'head'=2] {'seq'}, dimensions={1}, use_global_device_ids=true | all-gather | bytes 1032192 | tf_op jit(solution)/shard_map/all_gather | solution.py:152
  46.5 1.5 convolution_convert_fusion.7
  51.1 1.2 broadcast_compare_fusion.1
  54.0 1.1 reduce-scatter.7.cloned.1.call-done
  58.4 1.3 add_bitcast_fusion.1
  59.6 1.4 broadcast_compare_fusion
  61.1 20.8 %all-gather.1 = bf16[8,1,28]{2,1,0:T(2,128)(2,1)S(1)} all-gather(bf16[1,1,28]{2,1,0:T(2,128)(2,1)} %get-tuple-element.322), channel_id=1, replica_groups=mesh['section'=2,'seq'=8,'head'=2] {'seq'}, dimensions={0}, use_global_device_ids=true | all-gather | bytes 504 | tf_op jit(solution)/shard_map/all_gather | solution.py:18
  82.5 1.9 fusion.28
  87.9 20.1 %all-gather.5.cloned.1.call-done = bf16[8,28,4096]{2,1,0:T(8,128)(2,1)} async-done(((bf16[1,28,4096]{2,1,0:T(8,128)(2,1)}), bf16[8,28,4096]{2,1,0:T(8,128)(2,1)}) %all-gather.5.cloned.1.call-update) | async-done | bytes 1835024 | tf_op jit(solution)/shard_map/all_gather | solution.py:18
  108.0 14.4 %while.30 = (s32[]{:T(128)}, f32[28,4096]{1,0:T(8,128)S(1)}, s32[]{:T(128)}, bf16[8,28]{1,0:T(8,128)(2,1)}, bf16[8,28,4096]{2,1,0:T(8,128)(2,1)}, /*index=5*/s32[]{:T(128)}, s32[]{:T(128)}) while((s32[]{:T(128)}, f32[28,4096]{1,0:T(8,128)S(1)}, s32[]{:T(128)}, bf16[8,28]{1,0:T(8,128)(2,1)}, bf16[8,28,4096]{2,1,0:T(8,128)(2,1)}, ...), condition=%wide.region_3.5_spmd.clone, body=%wide.region_2.4_spmd.clone.sunk | while | flops 573472 | bytes 1147273 | solution.py:35
  108.6 1.1 fusion.116
  110.5 1.1 fusion.116
  115.9 1.1 fusion.116
  117.7 1.1 fusion.116
  121.3 1.1 fusion.116
  122.4 36.1 %all-gather.7.cloned.1.call-done = bf16[8,28,4096]{2,1,0:T(8,128)(2,1)} async-done(((bf16[1,28,4096]{2,1,0:T(8,128)(2,1)}), bf16[8,28,4096]{2,1,0:T(8,128)(2,1)}) %all-gather.7.cloned.1.call-update) | async-done | bytes 1835024 | tf_op jit(solution)/shard_map/all_gather | solution.py:41
  158.5 14.4 %while.31 = (s32[]{:T(128)}, f32[28,4096]{1,0:T(8,128)S(1)}, s32[]{:T(128)}, bf16[8,28,4096]{2,1,0:T(8,128)(2,1)}, bf16[8,28]{1,0:T(8,128)(2,1)}, /*index=5*/s32[]{:T(128)}, s32[]{:T(128)}, s32[]{:T(128)}, s32[]{:T(128)}) while((s32[]{:T(128)}, f32[28,4096]{1,0:T(8,128)S(1)}, s32[]{:T(128)}, bf16[8,28,4096]{2,1,0:T(8,128)(2,1)}, ...), condition=%wide.region_8.10_spmd.clone, body=%wide.region_7.9_spmd.clone.sunk | while | flops 573476 | bytes 1147335 | solution.py:59
  172.9 1.2 reshape.241
  175.2 1.5 multiply_reduce_fusion
  177.8 1.9 fusion.14
  179.9 1.2 copy.90
  181.1 2.3 fusion.26
  184.4 2.0 all_gather.24
  186.4 1.3 convolution_convert_fusion
  190.2 1.3 copy.100
  191.5 1.5 fusion.3
  193.0 1.3 collective-permute-start.1
  196.1 20.1 %all-reduce.4 = (f32[1,1792]{1,0:T(1,128)}, f32[1,28]{1,0:T(1,128)}, f32[1,28]{1,0:T(1,128)}, f32[1,28]{1,0:T(1,128)}) all-reduce(f32[1,1792]{1,0:T(1,128)S(1)} %broadcast_in_dim.73, f32[1,28]{1,0:T(1,128)S(1)} %get-tuple-element.329, f32[1,28]{1,0:T(1,128)S(1)} %get-tuple-element.328, ...), channel_id=1, replica_groups=mesh['section'=2,'seq'=8,'head'=2] {'seq'}, use_global_device_ids=true, to_apply=%region_15.17 | all-reduce | flops 1876 | bytes 15008 | tf_op jit(solution)/shard_map/psum | solution.py:219
  216.2 33.3 %reduce-scatter.5.cloned.1.call-done = bf16[32,1792]{1,0:T(8,128)(2,1)} async-done(((bf16[256,1792]{1,0:T(8,128)(2,1)}), bf16[32,1792]{1,0:T(8,128)(2,1)}) %reduce-scatter.5.cloned.1.call-update) | async-done | bytes 114704 | tf_op jit(solution)/shard_map/reduce_scatter | solution.py:211
  249.5 1.6 bitcast_convert_fusion.2
  (157 shorter events, 41.8 us)
Async XLA Ops:
  7.2 41.7 %copy-start = (bf16[1,128,1792]{2,1,0:T(8,128)(2,1)S(1)}, bf16[1,128,1792]{2,1,0:T(8,128)(2,1)}, u32[]{:S(2)}) copy-start(bf16[1,128,1792]{2,1,0:T(8,128)(2,1)} %param.13) | copy-start | bytes 1376260
  7.2 41.9 %copy-start.27 = (f32[1,28]{1,0:T(1,128)S(1)}, f32[1,28]{1,0:T(1,128)}, u32[]{:S(2)}) copy-start(f32[1,28]{1,0:T(1,128)} %param.19) | copy-start | bytes 340
  7.2 42.0 %copy-start.15 = (f32[1,1792]{1,0:T(1,128)S(1)}, f32[1,1792]{1,0:T(1,128)}, u32[]{:S(2)}) copy-start(f32[1,1792]{1,0:T(1,128)} %param.17) | copy-start | bytes 21508
  7.2 48.0 %reduce-scatter.7.cloned.1.call-start = ((), (), s32[]{:S(2)}) async-start(), calls=%async_computation.5 | async-start | bytes 98304
  8.5 41.3 %collective-permute-start = (s32[1]{0:T(128)}, s32[1]{0:T(128)}, u32[]{:S(2)}, u32[]{:S(2)}) collective-permute-start(s32[1]{0:T(128)} %bitcast.17), channel_id=1, source_target_pairs={{0,2},{2,4},{4,6},{6,8},{8,10},{10,12},{12,14},{1,3},{3,5},{5,7},{... | collective-permute-start | bytes 20 | tf_op jit(solution)/shard_map/ppermute | solution.py:12
  46.5 4.6 %copy-start.22 = (s32[1,128]{1,0:T(1,128)S(1)}, s32[1,128]{1,0:T(1,128)}, u32[]{:S(2)}) copy-start(s32[1,128]{1,0:T(1,128)} %param.14) | copy-start | bytes 1540
  46.5 5.8 %copy-start.23 = (f32[1,28]{1,0:T(1,128)S(1)}, f32[1,28]{1,0:T(1,128)}, u32[]{:S(2)}) copy-start(f32[1,28]{1,0:T(1,128)} %param.18) | copy-start | bytes 340
  48.8 59.2 %all-gather.5.cloned.1.call-start = ((), (), s32[]{:S(2)}) async-start(), calls=%async_computation.2 | async-start | bytes 2359296 | tf_op jit(solution)/shard_map/all_gather | solution.py:18
  49.1 33.3 %copy-start.2 = (bf16[1,128,1792]{1,2,0:T(8,128)(2,1)}, bf16[1,128,1792]{1,2,0:T(8,128)(2,1)S(1)}, u32[]{:S(2)}) copy-start(bf16[1,128,1792]{1,2,0:T(8,128)(2,1)S(1)} %copy.82) | copy-start | bytes 1376260
  49.1 9.0 %copy-start.6 = (bf16[1,128,1792]{2,1,0:T(8,128)(2,1)S(1)}, bf16[1,128,1792]{2,1,0:T(8,128)(2,1)}, u32[]{:S(2)}) copy-start(bf16[1,128,1792]{2,1,0:T(8,128)(2,1)} %param.15) | copy-start | bytes 1376260
  49.2 4.1 %copy-start.31 = (f32[28]{0:T(128)}, f32[28]{0:T(128)S(1)}, u32[]{:S(2)}) copy-start(f32[28]{0:T(128)S(1)} %negate_bitcast_fusion) | copy-start | bytes 340
  52.3 2.8 %copy-start.16 = (pred[128]{0:T(512)(128)(4,1)}, pred[128]{0:T(512)(128)(4,1)S(1)}, u32[]{:S(2)}) copy-start(pred[128]{0:T(512)(128)(4,1)S(1)} %get-tuple-element.312) | copy-start | bytes 388
  52.3 2.8 %copy-start.18 = (f32[128]{0:T(128)}, f32[128]{0:T(128)S(1)}, u32[]{:S(2)}) copy-start(f32[128]{0:T(128)S(1)} %get-tuple-element.313) | copy-start | bytes 1540
  56.3 28.8 %copy-start.7 = (bf16[128,128]{1,0:T(8,128)(2,1)S(1)}, bf16[128,128]{1,0:T(8,128)(2,1)}, u32[]{:S(2)}) copy-start(bf16[128,128]{1,0:T(8,128)(2,1)} %reduce-scatter.7.cloned.1.call-done) | copy-start | bytes 98308
  57.4 101.1 %all-gather.7.cloned.1.call-start = ((), (), s32[]{:S(2)}) async-start(), calls=%async_computation.3 | async-start | bytes 2359296 | tf_op jit(solution)/shard_map/all_gather | solution.py:41
  58.4 26.7 %copy-start.9 = (f32[128,28]{0,1:T(8,128)S(1)}, f32[128,28]{0,1:T(8,128)}, u32[]{:S(2)}) copy-start(f32[128,28]{0,1:T(8,128)} %get-tuple-element.326) | copy-start | bytes 43012
  87.8 161.7 %reduce-scatter.5.cloned.1.call-start = ((), (), s32[]{:S(2)}) async-start(), calls=%async_computation.4 | async-start | bytes 1032192 | tf_op jit(solution)/shard_map/reduce_scatter | solution.py:211
  174.8 2.9 %copy-start.3 = (bf16[1,128,1792]{1,2,0:T(8,128)(2,1)S(1)}, bf16[1,128,1792]{1,2,0:T(8,128)(2,1)}, u32[]{:S(2)}) copy-start(bf16[1,128,1792]{1,2,0:T(8,128)(2,1)} %copy-done.2) | copy-start | bytes 1376260
  175.2 2.5 copy-start.10
  183.4 3.0 %copy-start.1 = (bf16[1,128,1792]{2,1,0:T(8,128)(2,1)S(1)}, bf16[1,128,1792]{2,1,0:T(8,128)(2,1)}, u32[]{:S(2)}) copy-start(bf16[1,128,1792]{2,1,0:T(8,128)(2,1)} %param.13) | copy-start | bytes 1376260
  184.1 3.6 %copy-start.25 = (f32[28]{0:T(128)S(1)}, f32[28]{0:T(128)}, u32[]{:S(2)}) copy-start(f32[28]{0:T(128)} %multiply_reduce_fusion.2) | copy-start | bytes 340
  184.1 3.9 %copy-start.17 = (pred[128]{0:T(512)(128)(4,1)S(1)}, pred[128]{0:T(512)(128)(4,1)}, u32[]{:S(2)}) copy-start(pred[128]{0:T(512)(128)(4,1)} %copy-done.16) | copy-start | bytes 388
  184.1 3.9 %copy-start.19 = (f32[128]{0:T(128)S(1)}, f32[128]{0:T(128)}, u32[]{:S(2)}) copy-start(f32[128]{0:T(128)} %copy-done.18) | copy-start | bytes 1540
  184.2 3.9 %copy-start.21 = (f32[28]{0:T(128)S(1)}, f32[28]{0:T(128)}, u32[]{:S(2)}) copy-start(f32[28]{0:T(128)} %copy-done.20) | copy-start | bytes 340
  184.2 3.9 %copy-start.24 = (f32[1,28]{1,0:T(1,128)S(1)}, f32[1,28]{1,0:T(1,128)}, u32[]{:S(2)}) copy-start(f32[1,28]{1,0:T(1,128)} %param.18) | copy-start | bytes 340
  184.2 3.9 %copy-start.30 = (f32[128]{0:T(128)S(1)}, f32[128]{0:T(128)}, u32[]{:S(2)}) copy-start(f32[128]{0:T(128)} %copy-done.29) | copy-start | bytes 1540
  184.2 3.9 %copy-start.32 = (f32[28]{0:T(128)S(1)}, f32[28]{0:T(128)}, u32[]{:S(2)}) copy-start(f32[28]{0:T(128)} %copy-done.31) | copy-start | bytes 340
  184.4 4.4 %copy-start.8 = (f32[28,64]{1,0:T(8,128)S(1)}, f32[28,64]{1,0:T(8,128)}, u32[]{:S(2)}) copy-start(f32[28,64]{1,0:T(8,128)} %reshape_squeeze.10) | copy-start | bytes 21508
  184.4 4.4 %copy-start.33 = (f32[28]{0:T(128)S(1)}, f32[28]{0:T(128)}, u32[]{:S(2)}) copy-start(f32[28]{0:T(128)} %add_bitcast_fusion.1) | copy-start | bytes 340
  191.5 4.5 %copy-start.28 = (f32[1,28]{1,0:T(1,128)S(1)}, f32[1,28]{1,0:T(1,128)}, u32[]{:S(2)}) copy-start(f32[1,28]{1,0:T(1,128)} %param.19) | copy-start | bytes 340
  191.5 4.6 %copy-start.26 = (f32[28]{0:T(128)S(1)}, f32[28]{0:T(128)}, u32[]{:S(2)}) copy-start(f32[28]{0:T(128)} %reduce_sum.161) | copy-start | bytes 340
  193.0 23.2 %collective-permute-start.1 = (bf16[1,128,1792]{2,1,0:T(8,128)(2,1)S(1)}, bf16[1,128,1792]{2,1,0:T(8,128)(2,1)S(1)}, u32[]{:S(2)}, u32[]{:S(2)}) collective-permute-start(bf16[1,128,1792]{2,1,0:T(8,128)(2,1)S(1)} %fusion.3), channel_id=1, source_target_pairs={{16,0},{17,1},{18,2},{19,3},{20,4},{21,5},{22,6},{23,7},{24,8},{25... | collective-permute-start | bytes 1376264 | tf_op jit(solution)/shard_map/ppermute | solution.py:12
  (8 other events, 13.9 us)
Sparse Core Ops, SparseCore 0:
  48.9 6.2 reduce-scatter.6
  57.5 50.4 all-gather.4
  110.7 47.7 all-gather.6
  187.9 61.6 reduce-scatter.4
where the time goes:
time: 260 us; the launch traced here: 258 us
  waiting for transfers between devices  90.7 us (35%)
  blocking collectives  75.6 us (29%)
  other arithmetic  39.5 us (15%)
  matrix products  17.4 us (7%)
  between operations  15.5 us (6%)
  local copies, waits for them, and re-layouts  12.4 us (5%)
  starting transfers between devices  6.82 us (3%)
    all_gather x1, waiting for transfers between devices, entering_2(): lax.all_gather(part.astype(kind), axis)  36.1 us
    reduce_scatter x1, waiting for transfers between devices, shards(): lax.psum_scatter(lax.dot_general(mixer_full, bwd_flat, (((0,), (0,)), (()...  33.3 us
    all_gather x1, blocking collectives, shards(): full_weight = lax.all_gather(proj_weight[0], 'seq', axis=0, tiled=True)  32.6 us
    all_gather x1, blocking collectives, entering(): lax.all_gather(part.astype(kind), axis)  20.8 us
    psum x1, blocking collectives, shards(): lax.psum(((out_grads[2] + sum_grads[2]).reshape(channels_here), out_grads...  20.1 us
    all_gather x1, waiting for transfers between devices, entering(): lax.all_gather(part.astype(kind), axis)  20.1 us
    select_n x16, other arithmetic, lap(): return jax.tree.map(lambda a, b: jnp.where(reached, a, b), new, before)  17.4 us
    ppermute x2, starting transfers between devices, shifted(): return lax.ppermute(block, axis, route)  6.65 us
  transfers between devices with their start and end apart: 6, of which 4 were waited for; matrix products, arithmetic and copies ran while one was open for 14% of the time, Pallas kernels for 0%

commit v1 on v0

--- a/solution.py
+++ b/solution.py
@@ -149,7 +149,15 @@
     skip_heads = skip_gain[0]
     docs_bwd = bwd_docs[0]
     doc_before = shifted(docs_bwd[-1:], "seq", 1)[0]
-    full_weight = lax.all_gather(proj_weight[0], "seq", axis=0, tiled=True)
+    ways, here = (lax.axis_size("seq"), lax.axis_index("seq"))
+    grown, reach = (proj_weight[0], 1)
+    while reach < ways:
+        theirs = lax.ppermute(grown, "seq", [(d, d ^ reach) for d in range(ways)])
+        mine_first = jnp.concatenate([grown, theirs], axis=0)
+        theirs_first = jnp.concatenate([theirs, grown], axis=0)
+        grown = jnp.where(here & reach == 0, mine_first, theirs_first)
+        reach = 2 * reach
+    full_weight = grown
     partial_value = jnp.dot(bwd_flat, full_weight.T, preferred_element_type=jnp.float32)
     mixer_bwd = lax.psum_scatter(
         partial_value.astype(jnp.bfloat16), "head", scatter_dimension=1, tiled=True

time: 260 us -> 250 us (0.962)
  blocking collectives: 75.6 us -> 42.9 us
  waiting for transfers between devices: 90.7 us -> 122 us
  other arithmetic: 39.5 us -> 25.6 us
  starting transfers between devices: 6.82 us -> 12.4 us
    all_gather x1 -> x0, blocking collectives: 32.6 us -> none  [shards(): full_weight = lax.all_gather(proj_weight[0], 'seq', axis=0, tiled=True)]
    ppermute x0 -> x3, waiting for transfers between devices: none -> 20.1 us  [shards(): theirs = lax.ppermute(grown, 'seq', [(d, d ^ reach) for d in range(ways)])]
    all_gather x1, waiting for transfers between devices: 20.1 us -> 39.6 us  [entering(): lax.all_gather(part.astype(kind), axis)]
    all_gather x1, waiting for transfers between devices: 36.1 us -> 21.8 us  [entering_2(): lax.all_gather(part.astype(kind), axis)]
    ppermute x0 -> x3, starting transfers between devices: none -> 7.05 us  [shards(): theirs = lax.ppermute(grown, 'seq', [(d, d ^ reach) for d in range(ways)])]
    reduce_scatter x0 -> x1, waiting for transfers between devices: none -> 6.54 us  [shards(): lax.psum_scatter(partial_value.astype(jnp.bfloat16), 'head', scatter_dime...]
    convert_element_type x8, other arithmetic: 5.52 us -> 0.06 us  [lap(): part[k].astype(own.dtype)]
    convert_element_type x8, other arithmetic: 5.52 us -> 0.06 us  [lap(): part[at].astype(own.dtype)]
  transfers between devices with their start and end apart: 6 -> 9, of which waited for: 4 -> 6; matrix products, arithmetic and copies ran while one was open for 14% -> 12% of each run, Pallas kernels for 0% -> 0%
where the time goes in v1:
time: 250 us; the launch traced here: 249 us
  waiting for transfers between devices  122 us (49%)
  blocking collectives  42.9 us (17%)
  other arithmetic  25.6 us (10%)
  matrix products  18.5 us (7%)
  between operations  15.4 us (6%)
  starting transfers between devices  12.4 us (5%)
  local copies, waits for them, and re-layouts  11.7 us (5%)
    all_gather x1, waiting for transfers between devices, entering(): lax.all_gather(part.astype(kind), axis)  39.6 us
    reduce_scatter x1, waiting for transfers between devices, shards(): lax.psum_scatter(lax.dot_general(mixer_full, bwd_flat, (((0,), (0,)), (()...  33.6 us
    all_gather x1, waiting for transfers between devices, entering_2(): lax.all_gather(part.astype(kind), axis)  21.8 us
    all_gather x1, blocking collectives, entering(): lax.all_gather(part.astype(kind), axis)  20.7 us
    psum x1, blocking collectives, shards(): lax.psum(((out_grads[2] + sum_grads[2]).reshape(channels_here), out_grads...  20.1 us
    ppermute x3, waiting for transfers between devices, shards(): theirs = lax.ppermute(grown, 'seq', [(d, d ^ reach) for d in range(ways)])  20.1 us
    select_n x16, other arithmetic, lap(): return jax.tree.map(lambda a, b: jnp.where(reached, a, b), new, before)  17.5 us
    ppermute x3, starting transfers between devices, shards(): theirs = lax.ppermute(grown, 'seq', [(d, d ^ reach) for d in range(ways)])  7.05 us
  transfers between devices with their start and end apart: 9, of which 6 were waited for; matrix products, arithmetic and copies ran while one was open for 12% of the time, Pallas kernels for 0%

profile of v1, /device:TPU:0, one launch (start us, length us, event | category | flops | bytes accessed | tf_op | source)
XLA Modules:
  0.0 248.8 jit_solution(1066373262604198638)
XLA Ops:
  7.2 3.0 %collective-permute-start = (bf16[32,1792]{1,0:T(8,128)(2,1)}, bf16[32,1792]{1,0:T(8,128)(2,1)S(1)}, u32[]{:S(2)}, u32[]{:S(2)}) collective-permute-start(bf16[32,1792]{1,0:T(8,128)(2,1)} %bitcast.251), channel_id=1, source_target_pairs={{0,2},{2,0},{4,6},{6,4},{8,10},{10,8},{12,14},{14,12},{1,3},{3,1},... | collective-permute-start | bytes 344072 | tf_op jit(solution)/shard_map/ppermute | solution.py:155
  10.3 3.3 %collective-permute-done = bf16[32,1792]{1,0:T(8,128)(2,1)S(1)} collective-permute-done((bf16[32,1792]{1,0:T(8,128)(2,1)}, bf16[32,1792]{1,0:T(8,128)(2,1)S(1)}, u32[]{:S(2)}, u32[]{:S(2)}) %collective-permute-start) | collective-permute-done | bytes 114720 | tf_op jit(solution)/shard_map/ppermute | solution.py:155
  14.6 1.9 collective-permute-start.1
  16.5 1.2 slice.21
  17.7 3.9 %collective-permute-start.3 = (s32[1]{0:T(128)}, s32[1]{0:T(128)}, u32[]{:S(2)}, u32[]{:S(2)}) collective-permute-start(s32[1]{0:T(128)} %bitcast.18), channel_id=1, source_target_pairs={{0,2},{2,4},{4,6},{6,8},{8,10},{10,12},{12,14},{1,3},{3,5},{5,7},{... | collective-permute-start | bytes 20 | tf_op jit(solution)/shard_map/ppermute | solution.py:12
  22.5 1.3 copy.72
  23.8 2.2 collective-permute-start.2
  26.9 1.2 broadcast_compare_fusion.1
  28.2 16.7 %collective-permute-done.2 = bf16[128,1792]{1,0:T(8,128)(2,1)S(1)} collective-permute-done((bf16[128,1792]{1,0:T(8,128)(2,1)S(1)}, bf16[128,1792]{1,0:T(8,128)(2,1)S(1)}, u32[]{:S(2)}, u32[]{:S(2)}) %collective-permute-start.2) | collective-permute-done | bytes 458784 | tf_op jit(solution)/shard_map/ppermute | solution.py:155
  46.3 6.5 %reduce-scatter.3.cloned.1.call-done = bf16[128,128]{0,1:T(8,128)(2,1)} async-done(((bf16[128,256]{0,1:T(8,128)(2,1)}), bf16[128,128]{0,1:T(8,128)(2,1)}) %reduce-scatter.3.cloned.1.call-update) | async-done | bytes 32784 | tf_op jit(solution)/shard_map/reduce_scatter | solution.py:162
  52.8 1.3 fusion.25
  58.7 20.7 %all-gather = bf16[8,1,28]{2,1,0:T(2,128)(2,1)S(1)} all-gather(bf16[1,1,28]{2,1,0:T(2,128)(2,1)S(1)} %get-tuple-element.322), channel_id=1, replica_groups=mesh['section'=2,'seq'=8,'head'=2] {'seq'}, dimensions={0}, use_global_device_ids=true | all-gather | bytes 504 | tf_op jit(solution)/shard_map/all_gather | solution.py:18
  80.1 1.1 convolution_convert_fusion.3
  81.3 2.1 convert_element_type.243
  84.3 21.8 %all-gather.6.cloned.1.call-done = bf16[8,28,4096]{2,1,0:T(8,128)(2,1)} async-done(((bf16[1,28,4096]{2,1,0:T(8,128)(2,1)}), bf16[8,28,4096]{2,1,0:T(8,128)(2,1)}) %all-gather.6.cloned.1.call-update) | async-done | bytes 1835024 | tf_op jit(solution)/shard_map/all_gather | solution.py:41
  106.1 9.1 %while.31 = (s32[]{:T(128)}, f32[28,4096]{1,0:T(8,128)S(1)}, s32[]{:T(128)}, bf16[8,28,4096]{2,1,0:T(8,128)(2,1)}, bf16[8,28]{1,0:T(8,128)(2,1)S(1)}, /*index=5*/s32[]{:T(128)}, s32[]{:T(128)}, s32[]{:T(128)}, s32[]{:T(128)}) while((s32[]{:T(128)}, f32[28,4096]{1,0:T(8,128)S(1)}, s32[]{:T(128)}, bf16[8,28,4096]{2,1,0:T(8,128)(2,1)}, ...), condition=%wide.region_8.10_spmd.clone, body=%wide.region_7.9_spmd.clone.sunk | while | flops 573476 | bytes 1147335 | solution.py:59
  113.0 1.1 fusion.118
  114.1 1.1 fusion.118
  115.2 1.2 reshape.241
  116.4 39.6 %all-gather.4.cloned.1.call-done = bf16[8,28,4096]{2,1,0:T(8,128)(2,1)} async-done(((bf16[1,28,4096]{2,1,0:T(8,128)(2,1)}), bf16[8,28,4096]{2,1,0:T(8,128)(2,1)}) %all-gather.4.cloned.1.call-update) | async-done | bytes 1835024 | tf_op jit(solution)/shard_map/all_gather | solution.py:18
  156.1 9.0 %while.30 = (s32[]{:T(128)}, f32[28,4096]{1,0:T(8,128)S(1)}, s32[]{:T(128)}, bf16[8,28]{1,0:T(8,128)(2,1)S(1)}, bf16[8,28,4096]{2,1,0:T(8,128)(2,1)}, /*index=5*/s32[]{:T(128)}, s32[]{:T(128)}) while((s32[]{:T(128)}, f32[28,4096]{1,0:T(8,128)S(1)}, s32[]{:T(128)}, bf16[8,28]{1,0:T(8,128)(2,1)S(1)}, bf16[8,28,4096]{2,1,0:T(8,128)(2,1)}, ...), condition=%wide.region_3.5_spmd.clone, body=%wide.region_2.4_spmd.clone.sunk | while | flops 573472 | bytes 1147273 | solution.py:35
  166.2 1.4 multiply_reduce_fusion
  167.9 1.9 fusion.14
  169.9 1.2 copy.78
  171.1 1.7 fusion.78
  174.3 2.0 all_gather.20
  176.4 1.3 convolution_convert_fusion
  180.5 2.4 fusion.3
  182.9 1.3 collective-permute-start.4
  186.1 20.1 %all-reduce.4 = (f32[1,1792]{1,0:T(1,128)}, f32[1,28]{1,0:T(1,128)}, f32[1,28]{1,0:T(1,128)}, f32[1,28]{1,0:T(1,128)}) all-reduce(f32[1,1792]{1,0:T(1,128)S(1)} %broadcast_in_dim.73, f32[1,28]{1,0:T(1,128)S(1)} %get-tuple-element.329, f32[1,28]{1,0:T(1,128)S(1)} %get-tuple-element.328, ...), channel_id=1, replica_groups=mesh['section'=2,'seq'=8,'head'=2] {'seq'}, use_global_device_ids=true, to_apply=%region_15.17 | all-reduce | flops 1876 | bytes 15008 | tf_op jit(solution)/shard_map/psum | solution.py:227
  206.2 33.6 %reduce-scatter.5.cloned.1.call-done = bf16[32,1792]{1,0:T(8,128)(2,1)} async-done(((bf16[256,1792]{1,0:T(8,128)(2,1)}), bf16[32,1792]{1,0:T(8,128)(2,1)}) %reduce-scatter.5.cloned.1.call-update) | async-done | bytes 114704 | tf_op jit(solution)/shard_map/reduce_scatter | solution.py:219
  239.9 1.6 bitcast_convert_fusion.2
  (139 shorter events, 32.8 us)
Async XLA Ops:
  7.2 19.3 %copy-start.3 = (bf16[1,128,1792]{2,1,0:T(8,128)(2,1)S(1)}, bf16[1,128,1792]{2,1,0:T(8,128)(2,1)}, u32[]{:S(2)}) copy-start(bf16[1,128,1792]{2,1,0:T(8,128)(2,1)} %param.15) | copy-start | bytes 1376260
  7.2 45.6 %reduce-scatter.3.cloned.1.call-start = ((), (), s32[]{:S(2)}) async-start(), calls=%async_computation.2 | async-start | bytes 98304 | tf_op jit(solution)/shard_map/reduce_scatter | solution.py:162
  7.2 6.4 %collective-permute-start = (bf16[32,1792]{1,0:T(8,128)(2,1)}, bf16[32,1792]{1,0:T(8,128)(2,1)S(1)}, u32[]{:S(2)}, u32[]{:S(2)}) collective-permute-start(bf16[32,1792]{1,0:T(8,128)(2,1)} %bitcast.251), channel_id=1, source_target_pairs={{0,2},{2,0},{4,6},{6,4},{8,10},{10,8},{12,14},{14,12},{1,3},{3,1},... | collective-permute-start | bytes 344072 | tf_op jit(solution)/shard_map/ppermute | solution.py:155
  10.3 16.6 %copy-start.13 = (f32[1,28]{1,0:T(1,128)S(1)}, f32[1,28]{1,0:T(1,128)}, u32[]{:S(2)}) copy-start(f32[1,28]{1,0:T(1,128)} %param.19) | copy-start | bytes 340
  10.3 16.6 %copy-start.9 = (s32[1,128]{1,0:T(1,128)S(1)}, s32[1,128]{1,0:T(1,128)}, u32[]{:S(2)}) copy-start(s32[1,128]{1,0:T(1,128)} %param.14) | copy-start | bytes 1540
  10.3 34.6 %copy-start.1 = (bf16[1,128,1792]{2,1,0:T(8,128)(2,1)S(1)}, bf16[1,128,1792]{2,1,0:T(8,128)(2,1)}, u32[]{:S(2)}) copy-start(bf16[1,128,1792]{2,1,0:T(8,128)(2,1)} %param.13) | copy-start | bytes 1376260
  14.6 9.1 %collective-permute-start.1 = (bf16[64,1792]{1,0:T(8,128)(2,1)S(1)}, bf16[64,1792]{1,0:T(8,128)(2,1)S(1)}, u32[]{:S(2)}, u32[]{:S(2)}) collective-permute-start(bf16[64,1792]{1,0:T(8,128)(2,1)S(1)} %maximum_select_fusion.2), channel_id=1, source_target_pairs={{0,4},{2,6},{4,0},{6,2},{8,12},{10,14},{12,8},{14,10},{1,5},{3,7},... | collective-permute-start | bytes 688136 | tf_op jit(solution)/shard_map/ppermute | solution.py:155
  17.7 9.1 %collective-permute-start.3 = (s32[1]{0:T(128)}, s32[1]{0:T(128)}, u32[]{:S(2)}, u32[]{:S(2)}) collective-permute-start(s32[1]{0:T(128)} %bitcast.18), channel_id=1, source_target_pairs={{0,2},{2,4},{4,6},{6,8},{8,10},{10,12},{12,14},{1,3},{3,5},{5,7},{... | collective-permute-start | bytes 20 | tf_op jit(solution)/shard_map/ppermute | solution.py:12
  23.8 22.1 %copy-start.4 = (bf16[128,1792]{1,0:T(8,128)(2,1)}, bf16[128,1792]{1,0:T(8,128)(2,1)S(1)}, u32[]{:S(2)}) copy-start(bf16[128,1792]{1,0:T(8,128)(2,1)S(1)} %maximum_select_fusion.1) | copy-start | bytes 1376260
  23.8 21.0 %collective-permute-start.2 = (bf16[128,1792]{1,0:T(8,128)(2,1)S(1)}, bf16[128,1792]{1,0:T(8,128)(2,1)S(1)}, u32[]{:S(2)}, u32[]{:S(2)}) collective-permute-start(bf16[128,1792]{1,0:T(8,128)(2,1)S(1)} %maximum_select_fusion.1), channel_id=1, source_target_pairs={{0,8},{2,10},{4,12},{6,14},{8,0},{10,2},{12,4},{14,6},{1,9},{3,11}... | collective-permute-start | bytes 1376264 | tf_op jit(solution)/shard_map/ppermute | solution.py:155
  26.9 19.1 %copy-start.19 = (f32[28]{0:T(128)}, f32[28]{0:T(128)S(1)}, u32[]{:S(2)}) copy-start(f32[28]{0:T(128)S(1)} %negate_bitcast_fusion) | copy-start | bytes 340
  28.1 17.9 %copy-start.15 = (f32[128]{0:T(128)}, f32[128]{0:T(128)S(1)}, u32[]{:S(2)}) copy-start(f32[128]{0:T(128)S(1)} %get-tuple-element.323) | copy-start | bytes 1540
  28.1 17.9 %copy-start.10 = (f32[1,28]{1,0:T(1,128)S(1)}, f32[1,28]{1,0:T(1,128)}, u32[]{:S(2)}) copy-start(f32[1,28]{1,0:T(1,128)} %param.18) | copy-start | bytes 340
  44.9 1.1 copy-start.17
  45.9 9.7 %copy-start.18 = (f32[1,28]{1,0:T(1,128)S(1)}, f32[1,28]{1,0:T(1,128)}, u32[]{:S(2)}) copy-start(f32[1,28]{1,0:T(1,128)} %param.20) | copy-start | bytes 340
  45.9 60.2 %all-gather.6.cloned.1.call-start = ((), (), s32[]{:S(2)}) async-start(), calls=%async_computation.4 | async-start | bytes 2359296 | tf_op jit(solution)/shard_map/all_gather | solution.py:41
  54.4 25.7 %copy-start.6 = (bf16[128,128]{0,1:T(8,128)(2,1)S(1)}, bf16[128,128]{0,1:T(8,128)(2,1)}, u32[]{:S(2)}) copy-start(bf16[128,128]{0,1:T(8,128)(2,1)} %reduce-scatter.3.cloned.1.call-done) | copy-start | bytes 98308
  55.5 100.6 %all-gather.4.cloned.1.call-start = ((), (), s32[]{:S(2)}) async-start(), calls=%async_computation.3 | async-start | bytes 2359296 | tf_op jit(solution)/shard_map/all_gather | solution.py:18
  83.4 156.4 %reduce-scatter.5.cloned.1.call-start = ((), (), s32[]{:S(2)}) async-start(), calls=%async_computation.5 | async-start | bytes 1032192 | tf_op jit(solution)/shard_map/reduce_scatter | solution.py:219
  166.2 1.7 copy-start.7
  166.2 1.7 copy-start.8
  172.8 3.5 %copy-start.2 = (bf16[1,128,1792]{2,1,0:T(8,128)(2,1)S(1)}, bf16[1,128,1792]{2,1,0:T(8,128)(2,1)}, u32[]{:S(2)}) copy-start(bf16[1,128,1792]{2,1,0:T(8,128)(2,1)} %param.13) | copy-start | bytes 1376260
  173.0 4.7 %copy-start.11 = (f32[28]{0:T(128)S(1)}, f32[28]{0:T(128)}, u32[]{:S(2)}) copy-start(f32[28]{0:T(128)} %multiply_reduce_fusion.2) | copy-start | bytes 340
  174.0 4.0 %copy-start.16 = (f32[128]{0:T(128)S(1)}, f32[128]{0:T(128)}, u32[]{:S(2)}) copy-start(f32[128]{0:T(128)} %copy-done.15) | copy-start | bytes 1540
  174.0 4.0 %copy-start.20 = (f32[28]{0:T(128)S(1)}, f32[28]{0:T(128)}, u32[]{:S(2)}) copy-start(f32[28]{0:T(128)} %copy-done.19) | copy-start | bytes 340
  174.0 4.4 %copy-start.21 = (f32[28]{0:T(128)S(1)}, f32[28]{0:T(128)}, u32[]{:S(2)}) copy-start(f32[28]{0:T(128)} %add_bitcast_fusion.1) | copy-start | bytes 340
  178.4 1.0 copy-start
  179.5 1.0 copy-start.5
  180.5 5.6 %copy-start.14 = (f32[1,28]{1,0:T(1,128)S(1)}, f32[1,28]{1,0:T(1,128)}, u32[]{:S(2)}) copy-start(f32[1,28]{1,0:T(1,128)} %param.19) | copy-start | bytes 340
  180.5 5.6 %copy-start.12 = (f32[28]{0:T(128)S(1)}, f32[28]{0:T(128)}, u32[]{:S(2)}) copy-start(f32[28]{0:T(128)} %reduce_sum.161) | copy-start | bytes 340
  182.9 23.4 %collective-permute-start.4 = (bf16[1,128,1792]{2,1,0:T(8,128)(2,1)}, bf16[1,128,1792]{2,1,0:T(8,128)(2,1)S(1)}, u32[]{:S(2)}, u32[]{:S(2)}) collective-permute-start(bf16[1,128,1792]{2,1,0:T(8,128)(2,1)} %fusion.3), channel_id=1, source_target_pairs={{16,0},{17,1},{18,2},{19,3},{20,4},{21,5},{22,6},{23,7},{24,8},{25... | collective-permute-start | bytes 1376264 | tf_op jit(solution)/shard_map/ppermute | solution.py:12
Sparse Core Ops, SparseCore 0:
  46.1 6.7 reduce-scatter.2
  55.6 50.4 all-gather.5
  108.3 47.7 all-gather.3
  177.8 61.9 reduce-scatter.4
